TPU v7x, 512 devices: a whole 4x8x8 slice. The times are simulated.
512 devices in a mesh: gx: 8 (over y), gy: 64 (over z, x, core).
Axes of the slice: x: 4, y: 8, z: 8, core: 2. Of those that a mesh axis runs over, the one named last changes fastest.
Arguments:
- source: float32 [512, 256, 128], P('gy', 'gx'), may hold values from -0.004 to 0.004
- mask: int32 [512, 256, 128], P('gy', 'gx'), may hold values from 0 to 2, as said below
- cond_x: float32 [512, 256, 128], P('gy', 'gx'), may hold values from 0.0012 to 0.06
- cond_y: float32 [512, 256, 128], P('gy', 'gx'), may hold values from 0.4 to 5
- cond_z: float32 [512, 256, 128], P('gy', 'gx'), may hold values from 0.0004 to 0.01
Outputs:
- solution: float32 [512, 256, 128], P('gy', 'gx')
Inputs may be any that keep to these rules, and one draw needn't show every extreme that they name: `mask`: 0 marks a fluid cell, 1 a cut cell, 2 a solid cell.
All inputs are finite; a program needn't handle non-finite values.
Results may differ from a plain program's by a relative error of at most 0.00095.
Values sent between devices are 32-bit elements; how exact they have to be, the bound alone decides.
No kernel may reach another device: no remote copies, remote signals or barrier semaphores. Data moves between devices by JAX's collectives and lax.ppermute only.
A program may use at most 128 MiB of HBM per device.

v0:
```python
import jax
import jax.numpy as jnp
from jax import lax
from jax.sharding import Mesh
from jax.sharding import PartitionSpec as P

LEVELS = 6
GY = ("gy_0", "gy_1", "gy_2")
base_shift = 0.001
wall_term = 0.02


def in_blocks(x, dim, count):
    before, after = (x.shape[:dim], x.shape[dim + 1 :])
    return jnp.moveaxis(x.reshape(*before, count, -1, *after), dim, 0)


def in_order(parts, dim):
    parts = jnp.moveaxis(parts, 0, dim)
    shape = parts.shape
    return parts.reshape(*shape[:dim], shape[dim] * shape[dim + 1], *shape[dim + 2 :])


def turned_blocks(parts, axes, sequence):
    shape = [lax.axis_size(a) for a in axes]
    parts = parts.reshape(*shape, *parts.shape[1:])
    for k in sequence:
        parts = lax.all_to_all(parts, axes[k], split_axis=k, concat_axis=k, tiled=True)
    return parts.reshape(-1, *parts.shape[len(axes) :])


def exchange_by_chip(x, groups, sequence, split_dim, concat_dim):
    count = lax.axis_size(groups[0]) * lax.axis_size(groups[1])
    parts = in_blocks(x, split_dim, count)
    return in_order(turned_blocks(parts, groups, sequence), concat_dim)


def copy_for_each(x, axis):
    count = lax.axis_size(axis)
    return lax.all_to_all(jnp.broadcast_to(x[None], (count, *x.shape)), axis, 0, 0, tiled=True)


def gather_directly(x, axis, dim):
    parts = copy_for_each(x, axis)
    return in_order(parts, dim)


def padded(cells, sides, width):
    for axis, dim in sides:
        count = lax.axis_size(axis)
        ends = count - 1
        head = lax.slice_in_dim(cells, 0, width, axis=dim)
        tail = lax.slice_in_dim(cells, cells.shape[dim] - width, cells.shape[dim], axis=dim)
        cells = jnp.concatenate(
            [
                lax.ppermute(tail, axis, [(i, (i + 1) % count) for i in range(ends)]),
                cells,
                lax.ppermute(head, axis, [((i + 1) % count, i) for i in range(ends)]),
            ],
            axis=dim,
        )
    return cells


def with_halo(x, sides, width):
    edges = {}
    for axis, dim in sides:
        count, length = (lax.axis_size(axis), x.shape[dim])
        up = [(i, (i + 1) % count) for i in range(count - 1)]
        last = lax.slice_in_dim(x, length - width, length, axis=dim)
        leading = lax.slice_in_dim(x, 0, width, axis=dim)
        edges[dim] = (
            lax.ppermute(last, axis, up),
            lax.ppermute(leading, axis, [(b, a) for a, b in up]),
        )
    done = []
    for _, dim in sides:
        low, high = edges[dim]
        around = [(width, width) if d in done else (0, 0) for d in range(x.ndim)]
        x = jnp.concatenate([jnp.pad(low, around), x, jnp.pad(high, around)], axis=dim)
        done.append(dim)
    return x


def swapped(x, axis, stride):
    return lax.ppermute(x, axis, [(i, i ^ 1 << stride) for i in range(lax.axis_size(axis))])


def ahead(field, axis):
    size = field.shape[axis]
    edge = jnp.zeros_like(lax.slice_in_dim(field, 0, 1, axis=axis))
    return jnp.concatenate([lax.slice_in_dim(field, 1, size, axis=axis), edge], axis=axis)


def behind(field, axis):
    size = field.shape[axis]
    edge = jnp.zeros_like(lax.slice_in_dim(field, 0, 1, axis=axis))
    return jnp.concatenate([edge, lax.slice_in_dim(field, 0, size - 1, axis=axis)], axis=axis)


def coarse_sum(field):
    depth, width, height = field.shape
    return field.reshape(depth // 2, 2, width // 2, 2, height // 2, 2).sum(axis=(1, 3, 5))


def coarse_face(face, axis, parity):
    picked = lax.slice_in_dim(face, parity, face.shape[axis], stride=2, axis=axis)
    return 0.125 * coarse_sum(jnp.repeat(picked, 2, axis=axis))


def prolong(field):
    return jnp.repeat(jnp.repeat(jnp.repeat(field, 2, axis=0), 2, axis=1), 2, axis=2)


def upper_flag(bit):
    return lax.axis_index(GY) // 2**bit % 2


def line_factors(lower, diag, upper):
    denoms = [diag[0]]
    ratios = [upper[0] / diag[0]]
    for place in range(1, diag.shape[0]):
        pivot = diag[place] - lower[place] * ratios[place - 1]
        denoms.append(pivot)
        ratios.append(upper[place] / pivot)
    return (denoms, ratios)


def rows_solve(level, rhs):
    lower = level["lower"]
    denoms = level["denoms"]
    ratios = level["ratios"]
    count = rhs.shape[0]
    values = [rhs[0] / denoms[0]]
    for place in range(1, count):
        values.append((rhs[place] - lower[place] * values[place - 1]) / denoms[place])
    result = [values[count - 1]]
    for place in range(count - 2, -1, -1):
        result.append(values[place] - ratios[place] * result[-1])
    return jnp.stack(result[::-1])


def assemble(faces, group):
    face_x, low_x, face_y, low_y, face_z, shift = faces
    low_z = behind(face_z, 2)
    diag = shift + face_x + low_x + face_y + low_y + face_z + low_z
    level = {
        "face_x": face_x,
        "low_x": low_x,
        "face_y": face_y,
        "low_y": low_y,
        "face_z": face_z,
        "low_z": low_z,
        "diag": diag,
        "group": group,
    }
    level["lower"] = -low_y
    denoms, ratios = line_factors(-low_y, diag, -face_y)
    level["denoms"] = denoms
    level["ratios"] = ratios
    blank = jnp.zeros_like(diag)
    level["first_resp"] = rows_solve(level, blank.at[0].set(1.0))
    level["last_resp"] = rows_solve(level, blank.at[-1].set(1.0))
    level["alpha"] = low_y[0] * level["first_resp"][0]
    level["gamma"] = low_y[0] * level["first_resp"][-1]
    level["beta"] = face_y[-1] * level["last_resp"][0]
    level["delta"] = face_y[-1] * level["last_resp"][-1]
    return level


def forward_terms(alpha, beta, gamma, delta, head, tail):
    zeros = jnp.zeros_like(head)
    ones = jnp.ones_like(head)
    return (
        gamma * beta - alpha * delta,
        zeros,
        delta,
        gamma * head - alpha * tail,
        gamma,
        tail,
        -alpha,
        zeros,
        ones,
    )


def chain_forward(earlier, later):
    product = []
    for left_row in range(3):
        for column in range(3):
            product.append(
                later[3 * left_row] * earlier[column]
                + later[3 * left_row + 1] * earlier[3 + column]
                + later[3 * left_row + 2] * earlier[6 + column]
            )
    scale = product[8]
    return tuple((entry / scale for entry in product))


def chain_backward(earlier, later):
    return (later[0] + later[1] * earlier[0], later[1] * earlier[1])


def settle(alpha, beta, head, state):
    carry_q = state[2] / state[8]
    carry_p = state[5] / state[8]
    pivot = 1.0 - alpha * carry_q
    return ((head + alpha * carry_p) / pivot, beta / pivot, carry_q, carry_p)


def reduced_local(alpha, beta, gamma, delta, head, tail):
    zeros = jnp.zeros_like(head[:1])
    ones = jnp.ones_like(head[:1])
    identity = (ones, zeros, zeros, zeros, ones, zeros, zeros, zeros, ones)
    terms = forward_terms(alpha, beta, gamma, delta, head, tail)
    inclusive = lax.associative_scan(chain_forward, terms, axis=0)
    state = tuple(
        (jnp.concatenate([plain, entry[:-1]], axis=0) for plain, entry in zip(identity, inclusive))
    )
    start, slope, carry_q, carry_p = settle(alpha, beta, head, state)
    later = lax.associative_scan(chain_backward, (start, slope), reverse=True, axis=0)
    next_first = jnp.concatenate([later[0][1:], zeros], axis=0)
    first = start + slope * next_first
    return (carry_p + carry_q * first, next_first)


def pick_block(values, index, shape):
    return lax.dynamic_index_in_dim(values, index, 0, keepdims=False).reshape(shape)


def reduced_moved(level, head, tail):
    group = level["group"]
    shape = head.shape
    packed = jnp.stack(
        [level["alpha"], level["beta"], level["gamma"], level["delta"], head, tail]
    ).reshape(6, 1, -1)
    if group == 1:
        moved = exchange_by_chip(packed, (("gy_0", "gy_1"), "gy_2"), (1, 0), 2, 1)
        prev_last, next_first = reduced_local(
            moved[0], moved[1], moved[2], moved[3], moved[4], moved[5]
        )
        back = lax.all_to_all(
            jnp.stack([prev_last, next_first]), GY, split_axis=1, concat_axis=2, tiled=True
        )
        return (back[0, 0].reshape(shape), back[1, 0].reshape(shape))
    whole = gather_directly(packed, GY, 1)
    whole = whole.reshape(6, whole.shape[1] // group, group, -1)[:, :, 0]
    prev_last, next_first = reduced_local(
        whole[0], whole[1], whole[2], whole[3], whole[4], whole[5]
    )
    index = lax.axis_index(GY) // group
    return (pick_block(prev_last, index, shape), pick_block(next_first, index, shape))


def line_solve(level, rhs):
    local = rows_solve(level, rhs)
    prev_last, next_first = reduced_moved(level, local[0], local[-1])
    return (
        local
        + (level["low_y"][0] * prev_last)[None] * level["first_resp"]
        + (level["face_y"][-1] * next_first)[None] * level["last_resp"]
    )


def neighbour_terms(level, field):
    rim = padded(field, (("gx", 1),), 1)
    return (
        level["face_x"] * rim[:, 2:]
        + level["low_x"] * rim[:, :-2]
        + level["face_z"] * ahead(field, 2)
        + level["low_z"] * behind(field, 2)
    )


def relax(level, field, rhs):
    return line_solve(level, rhs + neighbour_terms(level, field))


WHOLE_FROM = 3


def gather_whole(block, depth):
    if depth == 2:
        axes, count = (("gx",) + GY, lax.axis_size(GY))
    else:
        axes, count = (("gx", "gy_0", "gy_1"), lax.axis_size(GY) // 2)
    parts = lax.all_gather(block, axes, axis=0)
    parts = parts.reshape(lax.axis_size("gx"), count, *block.shape)
    parts = jnp.moveaxis(parts, (0, 1), (3, 1))
    lead, rows, width, height = (block.shape[0], block.shape[1], block.shape[2], block.shape[3])
    return parts.reshape(lead, count * rows, lax.axis_size("gx") * width, height)


def whole_level(face_x, face_y, face_z, shift):
    low_x = behind(face_x, 1)
    low_y = behind(face_y, 0)
    low_z = behind(face_z, 2)
    diag = shift + face_x + low_x + face_y + low_y + face_z + low_z
    level = {
        "face_x": face_x,
        "low_x": low_x,
        "face_y": face_y,
        "low_y": low_y,
        "face_z": face_z,
        "low_z": low_z,
        "diag": diag,
        "lower": -low_y,
    }
    level["denoms"], level["ratios"] = line_factors(-low_y, diag, -face_y)
    return level


def whole_terms(level, field):
    return (
        level["face_x"] * ahead(field, 1)
        + level["low_x"] * behind(field, 1)
        + level["face_z"] * ahead(field, 2)
        + level["low_z"] * behind(field, 2)
    )


def whole_cycle(levels, depth, rhs):
    level = levels[depth]
    field = rows_solve(level, rhs)
    if depth == len(levels) - 1:
        return rows_solve(level, rhs + whole_terms(level, field))
    residual = whole_terms(level, field)
    correction = whole_cycle(levels, depth + 1, 0.25 * coarse_sum(residual))
    field = field + prolong(correction)
    return rows_solve(level, rhs + whole_terms(level, field))


def body(source, mask, cond_x, cond_y, cond_z):
    open_cells = (mask != 2).astype(jnp.float32)
    wall = (mask == 1).astype(jnp.float32)
    rim = with_halo(
        jnp.stack([cond_x * open_cells, cond_y * open_cells, open_cells]), (("gx", 2), (GY, 1)), 1
    )
    faces = (
        cond_x * open_cells * rim[2, 1:-1, 2:],
        rim[0, 1:-1, :-2] * open_cells,
        cond_y * open_cells * rim[2, 2:, 1:-1],
        rim[1, :-2, 1:-1] * open_cells,
        cond_z * open_cells * ahead(open_cells, 2),
        base_shift + wall_term * wall,
    )
    rhs = source * open_cells
    levels = []
    fields = []
    sources = []
    residual = rhs
    for depth in range(WHOLE_FROM):
        group = 1
        if depth > 0:
            face_x, low_x, face_y, low_y, face_z, shift = faces
            faces = (
                coarse_face(face_x, 1, 1),
                coarse_face(low_x, 1, 0),
                coarse_face(face_y, 0, 1),
                coarse_face(low_y, 0, 0),
                coarse_face(face_z, 2, 1),
                0.25 * coarse_sum(shift),
            )
            rhs = 0.25 * coarse_sum(residual)
            if depth >= 2:
                group = 2 ** (depth - 1)
                stacked = jnp.stack((rhs,) + faces)
                partner = swapped(stacked, GY, depth - 2)
                upper = upper_flag(depth - 2) == 1
                folded = jnp.concatenate(
                    [jnp.where(upper, partner, stacked), jnp.where(upper, stacked, partner)], axis=1
                )
                rhs = folded[0]
                faces = tuple((folded[place] for place in range(1, 7)))
        level = assemble(faces, group)
        field = line_solve(level, rhs)
        residual = neighbour_terms(level, field)
        levels.append(level)
        fields.append(field)
        sources.append(rhs)
    face_x, low_x, face_y, low_y, face_z, shift = faces
    coarse = jnp.stack(
        [
            coarse_face(face_x, 1, 1),
            coarse_face(face_y, 0, 1),
            coarse_face(face_z, 2, 1),
            0.25 * coarse_sum(shift),
        ]
    )
    whole = gather_whole(coarse, WHOLE_FROM)
    whole_rhs = gather_whole((0.25 * coarse_sum(residual))[None], WHOLE_FROM)[0]
    face_x, face_y, face_z, shift = (whole[0], whole[1], whole[2], whole[3])
    chain = [whole_level(face_x, face_y, face_z, shift)]
    for depth in range(WHOLE_FROM + 1, LEVELS):
        face_x = coarse_face(face_x, 1, 1)
        face_y = coarse_face(face_y, 0, 1)
        face_z = coarse_face(face_z, 2, 1)
        shift = 0.25 * coarse_sum(shift)
        chain.append(whole_level(face_x, face_y, face_z, shift))
    whole_correction = whole_cycle(chain, 0, whole_rhs)
    rows, width, height = coarse.shape[1:]
    spread = 2 ** max(WHOLE_FROM - 2, 0)
    correction = lax.dynamic_slice(
        whole_correction,
        (rows * (lax.axis_index(GY) // spread), width * lax.axis_index("gx"), 0),
        (rows, width, height),
    )
    for depth in range(WHOLE_FROM - 1, -1, -1):
        if depth < WHOLE_FROM - 1 and depth + 1 >= 2:
            half = correction.shape[0] // 2
            correction = lax.dynamic_slice_in_dim(correction, upper_flag(depth - 1) * half, half, 0)
        field = fields[depth] + prolong(correction)
        correction = relax(levels[depth], field, sources[depth])
    return correction


def solution(mesh):
    finer = Mesh(mesh.devices.reshape(mesh.shape["gx"], 8, 4, 2), ("gx", "gy_0", "gy_1", "gy_2"))
    return jax.shard_map(
        body,
        mesh=finer,
        in_specs=(
            P(GY, "gx", None),
            P(GY, "gx", None),
            P(GY, "gx", None),
            P(GY, "gx", None),
            P(GY, "gx", None),
        ),
        out_specs=P(GY, "gx", None),
        check_vma=False,
    )
```

profile of v0, /device:TPU:57, one launch (start us, length us, event | category | flops | bytes accessed | tf_op | source)
XLA Modules:
  0.0 2341.1 jit_solution(15719183095452096029)
XLA Ops:
  13.1 9.7 reshape.649
  39.6 14.6 all-to-all-start.1
  72.9 10.7 all-to-all-start.2
  83.7 9.4 all-to-all-done.2
  102.6 9.7 reshape.648
  118.2 5.5 all_to_all.87
  130.4 7.9 all-to-all-done.4
  144.6 5.4 all-to-all-start.5
  151.3 8.8 all-to-all-done.5
  176.4 514.1 %all-gather.1 = f32[1024,2,4,16]{3,2,1,0:T(4,128)S(1)} all-gather(f32[4,2,4,16]{3,2,1,0:T(4,128)S(1)} %pad_maximum_fusion.47), channel_id=3, replica_groups=mesh['gx'=8,'gy_0'=8,'gy_1'=4,'gy_2'=2] {'gx','gy_0','gy_1'}, dimensions={0}, use_global_device_ids=true | all-gather | bytes 526336 | tf_op jit(solution)/shard_map/all_gather | solution.py:287
  716.5 187.0 %all-to-all-start.6 = ((f32[64,6,1,256]{3,2,1,0:T(1,128)}), f32[64,6,1,256]{3,2,1,0:T(1,128)}, u32[]{:S(2)}, u32[]{:S(2)}) async-start(f32[64,6,1,256]{3,2,1,0:T(1,128)} %broadcast_in_dim.193), calls=%async_computation.6 | async-start | bytes 786432 | tf_op jit(solution)/shard_map/all_to_all | solution.py:40
  932.1 5.1 slice.7913
  1304.6 503.7 %all-gather = f32[512,4,16]{2,1,0:T(4,128)S(1)} all-gather(f32[2,4,16]{2,1,0:T(4,128)S(1)} %broadcast_multiply_fusion.16), channel_id=2, replica_groups=mesh['gx'=8,'gy_0'=8,'gy_1'=4,'gy_2'=2] {'gx','gy_0','gy_1'}, dimensions={0}, use_global_device_ids=true | all-gather | bytes 131584 | tf_op jit(solution)/shard_map/all_gather | solution.py:287
  1839.6 11.0 reshape.658
  1996.3 10.9 stack.311
  2020.7 185.1 %all-to-all-start.7 = ((f32[64,6,1,256]{3,2,1,0:T(1,128)}), f32[64,6,1,256]{3,2,1,0:T(1,128)S(1)}, u32[]{:S(2)}, u32[]{:S(2)}) async-start(f32[64,6,1,256]{3,2,1,0:T(1,128)} %broadcast_in_dim.222), calls=%async_computation.7 | async-start | bytes 786432 | tf_op jit(solution)/shard_map/all_to_all | solution.py:40
  2206.5 14.5 all-to-all-done.7
  2226.8 10.4 collective-permute-start.13
  2248.6 13.2 all_to_all.89
  2267.7 15.1 all_to_all.90
  2295.3 5.3 all_to_all.91
  2306.7 9.1 all-to-all-done.12
  2322.3 5.8 all-to-all-start.13
  2328.2 9.5 all-to-all-done.13
  (2785 shorter events, 749.5 us)
Async XLA Ops:
  2.1 25.4 %collective-permute-start.3 = (f32[3,1,32,128]{3,2,1,0:T(8,128)S(1)}, f32[3,1,32,128]{3,2,1,0:T(8,128)S(1)}, u32[]{:S(2)}, u32[]{:S(2)}) collective-permute-start(f32[3,1,32,128]{3,2,1,0:T(8,128)S(1)} %get-tuple-element.941), channel_id=1, source_target_pairs={{0,1},{1,2},{2,3},{3,4},{4,5},{5,6},{6,7},{7,8},{8,9},{9,10},{10,1... | collective-permute-start | bytes 147464 | tf_op jit(solution)/shard_map/ppermute | solution.py:73
  5.8 21.7 collective-permute-start.1
  7.1 20.4 collective-permute-start
  11.1 17.2 collective-permute-start.2
  39.6 25.8 %all-to-all-start.1 = ((f32[32,1,768]{2,1,0:T(1,128)}), f32[32,1,768]{2,1,0:T(1,128)}, u32[]{:S(2)}, u32[]{:S(2)}) async-start(f32[32,1,768]{2,1,0:T(1,128)} %reshape.749), calls=%async_computation.1 | async-start | bytes 196608 | tf_op jit(solution)/shard_map/all_to_all | solution.py:28
  72.9 20.1 all-to-all-start.2
  95.1 4.4 collective-permute-start.4
  98.1 4.4 collective-permute-start.5
  125.5 12.7 all-to-all-start.4
  144.6 15.5 all-to-all-start.5
  160.6 4.9 collective-permute-start.6
  164.2 4.6 collective-permute-start.7
  170.2 4.3 collective-permute-start.8
  716.5 252.0 %all-to-all-start.6 = ((f32[64,6,1,256]{3,2,1,0:T(1,128)}), f32[64,6,1,256]{3,2,1,0:T(1,128)}, u32[]{:S(2)}, u32[]{:S(2)}) async-start(f32[64,6,1,256]{3,2,1,0:T(1,128)} %broadcast_in_dim.193), calls=%async_computation.6 | async-start | bytes 786432 | tf_op jit(solution)/shard_map/all_to_all | solution.py:40
  1294.8 4.3 collective-permute-start.10
  2008.4 5.0 collective-permute-start.11
  2012.0 4.3 collective-permute-start.12
  2020.7 200.2 %all-to-all-start.7 = ((f32[64,6,1,256]{3,2,1,0:T(1,128)}), f32[64,6,1,256]{3,2,1,0:T(1,128)S(1)}, u32[]{:S(2)}, u32[]{:S(2)}) async-start(f32[64,6,1,256]{3,2,1,0:T(1,128)} %broadcast_in_dim.222), calls=%async_computation.7 | async-start | bytes 786432 | tf_op jit(solution)/shard_map/all_to_all | solution.py:40
  2226.8 11.9 collective-permute-start.13
  2237.1 4.6 collective-permute-start.14
  2285.1 5.0 collective-permute-start.15
  2288.7 4.4 collective-permute-start.16
  2302.6 13.2 all-to-all-start.12
  2322.3 15.3 all-to-all-start.13
  (240 other events, 8706.4 us)
where the time goes:
time: 2370 us; the launch traced here: 2340 us
  blocking collectives  1070 us (45%)
  local copies, waits for them, and re-layouts  494 us (21%)
  starting transfers between devices  464 us (20%)
  other arithmetic  229 us (10%)
  waiting for transfers between devices  78.1 us (3%)
    all_gather x2, blocking collectives, gather_whole(): parts = lax.all_gather(block, axes, axis=0)  1020 us
    all_to_all x2, starting transfers between devices, copy_for_each(): lax.all_to_all(jnp.broadcast_to(x[None], (count, *x.shape)), axis, 0, 0,...  372 us
    slice x706, local copies, waits for them, and re-layouts, reduced_local(): inclusive = lax.associative_scan(chain_forward, terms, axis=0)  139 us
  transfers between devices with their start and end apart: 25, of which 13 were waited for; matrix products, arithmetic and copies ran while one was open for 4% of the time, Pallas kernels for 0%

commit v1 on v0

--- a/solution.py
+++ b/solution.py
@@ -239,9 +239,10 @@
         prev_last, next_first = reduced_local(
             moved[0], moved[1], moved[2], moved[3], moved[4], moved[5]
         )
-        back = lax.all_to_all(
-            jnp.stack([prev_last, next_first]), GY, split_axis=1, concat_axis=2, tiled=True
-        )
+        value = jnp.stack([prev_last, next_first])
+        cells_2 = jnp.split(value, lax.axis_size(GY), axis=1)
+        received = lax.all_to_all(jnp.stack(cells_2), GY, 0, 0)
+        back = jnp.concatenate(received, axis=2)
         return (back[0, 0].reshape(shape), back[1, 0].reshape(shape))
     whole = gather_directly(packed, GY, 1)
     whole = whole.reshape(6, whole.shape[1] // group, group, -1)[:, :, 0]

time: 2370 us -> 2410 us (1.017)
  local copies, waits for them, and re-layouts: 494 us -> 532 us
    unnamed x637 -> x889, local copies, waits for them, and re-layouts: 30.6 us -> 68.2 us
where the time goes in v1:
time: 2410 us; the launch traced here: 2380 us
  blocking collectives  1060 us (44%)
  local copies, waits for them, and re-layouts  532 us (22%)
  starting transfers between devices  465 us (19%)
  other arithmetic  233 us (10%)
  waiting for transfers between devices  78.4 us (3%)
    all_gather x2, blocking collectives, gather_whole(): parts = lax.all_gather(block, axes, axis=0)  1020 us
    all_to_all x2, starting transfers between devices, copy_for_each(): lax.all_to_all(jnp.broadcast_to(x[None], (count, *x.shape)), axis, 0, 0,...  372 us
    slice x706, local copies, waits for them, and re-layouts, reduced_local(): inclusive = lax.associative_scan(chain_forward, terms, axis=0)  139 us
    unnamed x889, local copies, waits for them, and re-layouts  68.2 us
  transfers between devices with their start and end apart: 25, of which 13 were waited for; matrix products, arithmetic and copies ran while one was open for 4% of the time, Pallas kernels for 0%

profile of v1, /device:TPU:57, one launch (start us, length us, event | category | flops | bytes accessed | tf_op | source)
XLA Modules:
  0.0 2383.4 jit_solution(12927642531898436762)
XLA Ops:
  13.1 9.8 reshape.646
  39.9 14.6 all-to-all-start.1
  74.1 10.7 all-to-all-start.2
  84.8 9.4 all-to-all-done.2
  103.9 9.8 reshape.645
  119.6 5.5 all_to_all.71
  131.9 7.8 all-to-all-done.4
  183.8 5.5 all-to-all-start.5
  190.5 8.8 all-to-all-done.5
  215.6 514.1 %all-gather.1 = f32[1024,2,4,16]{3,2,1,0:T(4,128)S(1)} all-gather(f32[4,2,4,16]{3,2,1,0:T(4,128)S(1)} %pad_maximum_fusion.45), channel_id=3, replica_groups=mesh['gx'=8,'gy_0'=8,'gy_1'=4,'gy_2'=2] {'gx','gy_0','gy_1'}, dimensions={0}, use_global_device_ids=true | all-gather | bytes 526336 | tf_op jit(solution)/shard_map/all_gather | solution.py:288
  755.7 187.6 %all-to-all-start.6 = ((f32[64,6,1,256]{3,2,1,0:T(1,128)}), f32[64,6,1,256]{3,2,1,0:T(1,128)}, u32[]{:S(2)}, u32[]{:S(2)}) async-start(f32[64,6,1,256]{3,2,1,0:T(1,128)} %broadcast_in_dim.193), calls=%async_computation.6 | async-start | bytes 786432 | tf_op jit(solution)/shard_map/all_to_all | solution.py:40
  971.8 5.1 slice.7909
  1343.4 503.3 %all-gather = f32[512,4,16]{2,1,0:T(4,128)S(1)} all-gather(f32[2,4,16]{2,1,0:T(4,128)S(1)} %broadcast_multiply_fusion.16), channel_id=2, replica_groups=mesh['gx'=8,'gy_0'=8,'gy_1'=4,'gy_2'=2] {'gx','gy_0','gy_1'}, dimensions={0}, use_global_device_ids=true | all-gather | bytes 131584 | tf_op jit(solution)/shard_map/all_gather | solution.py:288
  1877.9 11.1 reshape.656
  2034.5 10.9 stack.1586
  2058.9 184.8 %all-to-all-start.7 = ((f32[64,6,1,256]{3,2,1,0:T(1,128)}), f32[64,6,1,256]{3,2,1,0:T(1,128)S(1)}, u32[]{:S(2)}, u32[]{:S(2)}) async-start(f32[64,6,1,256]{3,2,1,0:T(1,128)} %broadcast_in_dim.222), calls=%async_computation.7 | async-start | bytes 786432 | tf_op jit(solution)/shard_map/all_to_all | solution.py:40
  2244.5 14.5 all-to-all-done.7
  2264.7 10.6 collective-permute-start.13
  2286.9 13.2 all_to_all.73
  2308.8 15.1 all_to_all.74
  2336.3 5.3 all_to_all.75
  2347.9 9.4 all-to-all-done.12
  2364.8 5.4 all-to-all-start.13
  2370.3 9.5 all-to-all-done.13
  (3071 shorter events, 790.4 us)
Async XLA Ops:
  2.1 25.5 %collective-permute-start.3 = (f32[3,1,32,128]{3,2,1,0:T(8,128)S(1)}, f32[3,1,32,128]{3,2,1,0:T(8,128)S(1)}, u32[]{:S(2)}, u32[]{:S(2)}) collective-permute-start(f32[3,1,32,128]{3,2,1,0:T(8,128)S(1)} %get-tuple-element.1067), channel_id=1, source_target_pairs={{0,1},{1,2},{2,3},{3,4},{4,5},{5,6},{6,7},{7,8},{8,9},{9,10},{10,1... | collective-permute-start | bytes 147464 | tf_op jit(solution)/shard_map/ppermute | solution.py:73
  5.8 21.8 collective-permute-start.1
  7.1 20.5 collective-permute-start
  11.1 17.3 collective-permute-start.2
  39.9 25.8 %all-to-all-start.1 = ((f32[32,1,768]{2,1,0:T(1,128)}), f32[32,1,768]{2,1,0:T(1,128)}, u32[]{:S(2)}, u32[]{:S(2)}) async-start(f32[32,1,768]{2,1,0:T(1,128)} %reshape.877), calls=%async_computation.1 | async-start | bytes 196608 | tf_op jit(solution)/shard_map/all_to_all | solution.py:28
  74.1 20.1 all-to-all-start.2
  96.4 4.4 collective-permute-start.4
  99.4 4.4 collective-permute-start.5
  127.0 12.7 all-to-all-start.4
  183.8 15.6 all-to-all-start.5
  199.9 4.9 collective-permute-start.6
  203.4 4.6 collective-permute-start.7
  209.5 4.3 collective-permute-start.8
  755.7 252.5 %all-to-all-start.6 = ((f32[64,6,1,256]{3,2,1,0:T(1,128)}), f32[64,6,1,256]{3,2,1,0:T(1,128)}, u32[]{:S(2)}, u32[]{:S(2)}) async-start(f32[64,6,1,256]{3,2,1,0:T(1,128)} %broadcast_in_dim.193), calls=%async_computation.6 | async-start | bytes 786432 | tf_op jit(solution)/shard_map/all_to_all | solution.py:40
  1333.5 4.3 collective-permute-start.10
  2046.6 5.0 collective-permute-start.11
  2050.2 4.3 collective-permute-start.12
  2058.9 200.0 %all-to-all-start.7 = ((f32[64,6,1,256]{3,2,1,0:T(1,128)}), f32[64,6,1,256]{3,2,1,0:T(1,128)S(1)}, u32[]{:S(2)}, u32[]{:S(2)}) async-start(f32[64,6,1,256]{3,2,1,0:T(1,128)} %broadcast_in_dim.222), calls=%async_computation.7 | async-start | bytes 786432 | tf_op jit(solution)/shard_map/all_to_all | solution.py:40
  2264.7 12.2 collective-permute-start.13
  2275.4 4.6 collective-permute-start.14
  2326.1 5.0 collective-permute-start.15
  2329.8 4.4 collective-permute-start.16
  2343.8 13.5 all-to-all-start.12
  2364.8 14.9 all-to-all-start.13
  (240 other events, 9495.8 us)
